TPU v7x, 32 devices: a whole 2x2x4 slice. The times are simulated.
32 devices in a mesh: groups: 2 (over y), queue: 4 (over z), dp: 4 (over x, core).
Axes of the slice: x: 2, y: 2, z: 4, core: 2. Of those that a mesh axis runs over, the one named last changes fastest.
Arguments:
- query_inputs: bfloat16 [8192, 1024], P(('groups', 'queue', 'dp')), parts along dimension 0, may hold values from -30 to 30
- key_inputs: bfloat16 [512, 1024], P(('groups', 'queue', 'dp')), parts along dimension 0, may hold values from -6 to 6
- query_weight: bfloat16 [1024, 1024], replicated, may hold values from -4 to 4
- key_weight: bfloat16 [1024, 1024], replicated, may hold values from -0.1875 to 0.1875
- queue_keys: bfloat16 [2048, 1024], P(('groups', 'queue')), parts along dimension 0, may hold values from -2 to 2
- write_pointer: int32 [2], P('groups'), parts along dimension 0, may hold values from 0 to 255
- slot_owner: int32 [32], P('groups'), parts along dimension 0, may hold values from 0 to 15, each once
- positive_index: int32 [8192], P(('groups', 'queue', 'dp')), parts along dimension 0, may hold values from 0 to 1023
Outputs:
- loss: float32 [8192], P(('groups', 'queue', 'dp')), parts along dimension 0
- query_weight_grad: float32 [2048, 1024], P(('groups', 'queue', 'dp')), parts along dimension 0
- new_queue: bfloat16 [2048, 1024], P(('groups', 'queue')), parts along dimension 0
There are 2 independent parts, one for each index of `groups`. A program takes and returns all parts, laid end to end along the dimension named above; an argument that names none is the same for every part. Nothing has to cross between parts.
Inputs may be any that keep to these rules, and one draw needn't show every extreme that they name: slot_owner is a permutation of 0 to 15.
All inputs are finite; a program needn't handle non-finite values.
Results may differ from a plain program's by a relative error of at most 0.0075.
Values may be sent and summed in bfloat16 or wider, within the bound.
No kernel may reach another device: no remote copies, remote signals or barrier semaphores. Data moves between devices by JAX's collectives and lax.ppermute only.
A program may use at most 192 MiB of HBM per device.

v0:
```python
import jax
import jax.numpy as jnp
from jax import lax
from jax.sharding import PartitionSpec as P

temper = 0.05


def make_fold(units, mapped):

    def fold(carry, piece, start):
        top, total, mixture, chosen = carry
        scores = (
            lax.dot_general(
                units, piece, (((1,), (1,)), ((), ())), preferred_element_type=jnp.float32
            )
            / temper
        )
        new_top = jnp.maximum(top, jnp.max(scores, -1))
        expo = jnp.exp(scores - new_top[:, None])
        total = jnp.sum(expo, -1)
        mixture = jnp.dot(expo.astype(jnp.bfloat16), piece, preferred_element_type=jnp.float32)
        count = piece.shape[0]
        hit = (mapped >= 0) & (mapped < count)
        picked = jnp.take(piece, jnp.clip(mapped, 0, count - 1), axis=0).astype(jnp.float32)
        chosen = jnp.where(hit[:, None], picked, 0.0)
        return (new_top, total, mixture, chosen)

    return fold


def start_carry(count, width):
    return (
        jnp.full((count,), -1e30, jnp.float32),
        jnp.zeros((count,), jnp.float32),
        jnp.zeros((count, width), jnp.float32),
        jnp.zeros((count, width), jnp.float32),
    )


def body(
    query_inputs,
    key_inputs,
    query_weight,
    key_weight,
    queue_keys,
    write_pointer,
    slot_owner,
    positive_index,
):
    q_dev, width = query_inputs.shape
    k_dev = queue_keys.shape[0]
    new_dev = key_inputs.shape[0]
    n_dp = lax.axis_size("dp")
    query = jnp.dot(query_inputs, query_weight, preferred_element_type=jnp.float32)
    inv_len = lax.rsqrt(jnp.sum(query * query, -1, keepdims=True) + 1e-06)
    unit_f = query * inv_len
    unit = unit_f.astype(jnp.bfloat16)
    fold = make_fold(unit, positive_index)
    top, total, mixture, chosen = fold(
        start_carry(q_dev, width),
        lax.all_gather(queue_keys, "queue", axis=0, tiled=True),
        jnp.int32(0),
    )
    mixture = mixture / total[:, None]
    positive = jnp.sum(unit.astype(jnp.float32) * chosen, -1) / temper
    loss = top + jnp.log(total) - positive
    grad_unit = (mixture - chosen) / temper
    grad_query = (
        (grad_unit - unit_f * jnp.sum(unit_f * grad_unit, -1, keepdims=True)) * inv_len
    ).astype(jnp.bfloat16)
    n_all = lax.axis_size(("queue", "dp"))
    share = width // n_all
    term = lax.dot_general(
        query_inputs, grad_query, (((0,), (0,)), ((), ())), preferred_element_type=jnp.float32
    )
    summed = lax.psum(term, ("queue", "dp"))
    grad_rows = lax.dynamic_slice_in_dim(summed, lax.axis_index(("queue", "dp")) * share, share, 0)
    fresh = jnp.dot(key_inputs, key_weight, preferred_element_type=jnp.float32)
    fresh = (fresh * lax.rsqrt(jnp.sum(fresh * fresh, -1, keepdims=True) + 1e-06)).astype(
        jnp.bfloat16
    )
    arrived = lax.all_gather(fresh, ("queue", "dp"), axis=0, tiled=True)
    n_blocks = slot_owner.shape[0]
    slots_here = lax.axis_index("queue") * n_dp + jnp.arange(n_dp, dtype=jnp.int32)
    match = slot_owner[None, :] == slots_here[:, None]
    owner_block = jnp.sum(jnp.where(match, jnp.arange(n_blocks, dtype=jnp.int32)[None, :], 0), -1)
    offset = (jnp.arange(k_dev, dtype=jnp.int32) - write_pointer[0]) % k_dev
    live = offset < n_dp * new_dev
    sub_block = jnp.minimum(offset // new_dev, n_dp - 1)
    source = jnp.take(owner_block, sub_block) * new_dev + offset % new_dev
    new_queue = jnp.where(live[:, None], jnp.take(arrived, source, axis=0), queue_keys)
    return (loss, grad_rows, new_queue)


def solution(mesh):
    in_specs = (
        P(("groups", "queue", "dp"), None),
        P(("groups", "queue", "dp"), None),
        P(),
        P(),
        P(("groups", "queue"), None),
        P("groups"),
        P("groups"),
        P(("groups", "queue", "dp")),
    )
    out_specs = (
        P(("groups", "queue", "dp")),
        P(("groups", "queue", "dp"), None),
        P(("groups", "queue"), None),
    )
    return jax.shard_map(body, mesh=mesh, in_specs=in_specs, out_specs=out_specs, check_vma=False)
```

profile of v0, /device:TPU:0, one launch (start us, length us, event | category | flops | bytes accessed | tf_op | source)
XLA Modules:
  0.0 193.4 jit_solution(15796007540766359770)
XLA Ops:
  7.2 0.0 copy-start
  7.2 0.0 all-gather.2.cloned.1.call-start
  7.2 0.7 all-gather.2.cloned.1.call-update
  7.9 0.0 all-reduce.2.cloned.1.call-start
  8.6 0.7 compare_select_fusion.9
  9.3 0.7 compare_and_fusion.1
  10.0 0.0 copy-done
  10.0 1.8 multiply_reduce_fusion.2
  11.9 46.1 %all-gather.2.cloned.1.call-done = bf16[1024,1024]{1,0:T(8,128)(2,1)} async-done(((bf16[256,1024]{1,0:T(8,128)(2,1)}), bf16[1024,1024]{1,0:T(8,128)(2,1)}) %all-gather.2.cloned.1.call-update) | async-done | bytes 2097168 | tf_op jit(solution)/shard_map/all_gather | solution.py:62
  58.0 2.4 %fusion.14 = (f32[256]{0:T(256)S(1)}, f32[256,1024]{1,0:T(8,128)S(1)}) fusion(bf16[1024,1024]{1,0:T(8,128)(2,1)} %all-gather.2.cloned.1.call-done, f32[256,1024]{1,0:T(8,128)S(1)} %get-tuple-element.23, f32[256]{0:T(256)S(1)} %add_rsqrt_fusion), kind=kOutput, calls=%fused_computation.68 | convolution fusion | flops 537919232 | bytes 4196352 | tf_op jit(solution)/shard_map/dot_general | solution.py:14
  60.4 0.0 copy-start.1
  60.4 1.0 copy-done.1
  61.4 0.3 fusion.3
  61.7 4.2 %gather_fusion = bf16[256,1024]{1,0:T(8,128)(2,1)} fusion(bf16[1024,1024]{1,0:T(8,128)(2,1)} %all-gather.2.cloned.1.call-done, s32[1024]{0:T(1024)S(1)} %pad_clamp_fusion.1), kind=kCustom, calls=%fused_computation | custom fusion | bytes 1049600 | tf_op jit(solution)/shard_map/jit(_take)/gather | solution.py:25
  65.9 0.0 copy-start.2
  65.9 3.1 %multiply_reduce_fusion = (f32[256]{0:T(256)S(1)}, f32[256]{0:T(256)S(1)}, f32[256,1024]{1,0:T(8,128)S(1)}) fusion(f32[256,1024]{1,0:T(8,128)S(1)} %get-tuple-element.23, f32[256]{0:T(256)S(1)} %add_rsqrt_fusion, bf16[256,1024]{1,0:T(8,128)(2,1)} %gather_fusion, pred[256]{0:T(512)(128)(4,1)S(1)} %get-tuple-element.16, ...), kind=kOutput, calls=%fused_computation.8 | convolution fusion | flops 540802560 | bytes 5772800 | tf_op jit(solution)/shard_map/dot_general | solution.py:22
  69.0 0.0 copy-done.2
  69.0 3.0 %convolution_bitcast_fusion = f32[1024,1024]{0,1:T(8,128)} fusion(bf16[256,1024]{1,0:T(8,128)(2,1)S(1)} %copy-done.2, f32[256,1024]{1,0:T(8,128)S(1)} %get-tuple-element.26, f32[256,1024]{1,0:T(8,128)S(1)} %get-tuple-element.23, f32[256]{0:T(256)S(1)} %get-tuple-element.12, f32[256]{0:T(256)S(1)} %add_rsqrt_fusion), kind=kOutput, calls=%fused_computation.2 | convolution fusion | flops 538181632 | bytes 6817792 | tf_op jit(solution)/shard_map/dot_general | solution.py:74
  72.0 0.0 copy-start.4
  72.0 0.0 copy-start.3
  72.0 0.0 all-reduce.2.cloned.1.call-update
  72.0 0.6 copy-done.4
  72.6 0.2 select_reduce_fusion
  72.8 0.6 fusion.13
  73.4 2.5 %compare_select_fusion = (s32[256,1]{0,1:T(1,128)S(1)}, s32[256,1]{0,1:T(1,128)S(1)}) fusion(s32[]{:T(128)} %bitcast.16, s32[]{:T(128)} %bitcast.5, s32[]{:T(128)} %bitcast.4, s32[]{:T(128)} %bitcast.3, s32[]{:T(128)} %bitcast.2), kind=kLoop, calls=%fused_computation.23 | loop fusion | flops 12800 | bytes 2068 | tf_op jit(solution)/shard_map/jit(_take)/jit(_where)/select_n | solution.py:92
  76.0 0.0 copy-done.3
  76.0 2.2 %multiply_reduce_fusion.3 = (f32[16]{0:T(128)S(1)}, f32[16,1024]{1,0:T(8,128)S(1)}) fusion(bf16[16,1024]{1,0:T(8,128)(2,1)S(1)} %copy-done.3, bf16[1024,1024]{1,0:T(8,128)(2,1)} %param.11), kind=kOutput, calls=%fused_computation.22 | convolution fusion | flops 33587184 | bytes 2195520 | tf_op jit(solution)/shard_map/dot_general | solution.py:79
  78.2 0.1 multiply_convert_fusion.3
  78.3 23.5 %all_gather.7 = bf16[256,1024]{1,0:T(8,128)(2,1)S(1)} all-gather(bf16[16,1024]{1,0:T(8,128)(2,1)S(1)} %multiply_convert_fusion.3), channel_id=1, replica_groups=mesh['groups'=2,'queue'=4,'dp'=4] {'queue','dp'}, dimensions={0}, use_global_device_ids=true | all-gather | bytes 557056 | tf_op jit(solution)/shard_map/all_gather | solution.py:83
  101.8 1.2 gather_fusion.1
  103.0 2.0 %select_select_fusion = bf16[256,1024]{1,0:T(8,128)(2,1)} fusion(bf16[256,1024]{1,0:T(8,128)(2,1)} %param.12, bf16[256,1024]{1,0:T(8,128)(2,1)S(1)} %gather_fusion.1, pred[256]{0:T(512)(128)(4,1)S(1)} %get-tuple-element.29, pred[256]{0:T(512)(128)(4,1)S(1)} %get-tuple-element.30), kind=kLoop, calls=%fused_computation.16 | loop fusion | flops 524288 | bytes 1573376 | tf_op jit(solution)/shard_map/jit(_where)/select_n | solution.py:92
  105.0 0.6 multiply_subtract_fusion
  105.6 78.9 %all-reduce.2.cloned.1.call-done = f32[1024,1024]{0,1:T(8,128)} async-done(((f32[1024,1024]{0,1:T(8,128)}), f32[1024,1024]{0,1:T(8,128)}) %all-reduce.2.cloned.1.call-update) | async-done | bytes 4194320 | tf_op jit(solution)/shard_map/psum | solution.py:77
  184.5 1.2 constant_dynamic-slice_fusion
  185.7 0.9 copy.13
  (7 shorter events, 0.1 us)
Async XLA Ops:
  7.2 2.8 %copy-start = (bf16[1024,1024]{1,0:T(8,128)(2,1)S(1)}, bf16[1024,1024]{1,0:T(8,128)(2,1)}, u32[]{:S(2)}) copy-start(bf16[1024,1024]{1,0:T(8,128)(2,1)} %param.10) | copy-start | bytes 6291460
  7.2 50.8 %all-gather.2.cloned.1.call-start = ((), (), s32[]{:S(2)}) async-start(), calls=%async_computation | async-start | bytes 2621440 | tf_op jit(solution)/shard_map/all_gather | solution.py:62
  7.9 176.6 %all-reduce.2.cloned.1.call-start = ((), (), s32[]{:S(2)}) async-start(), calls=%async_computation.1 | async-start | bytes 8388608 | tf_op jit(solution)/shard_map/psum | solution.py:77
  60.4 1.0 copy-start.1
  65.9 3.1 %copy-start.2 = (bf16[256,1024]{1,0:T(8,128)(2,1)S(1)}, bf16[256,1024]{1,0:T(8,128)(2,1)}, u32[]{:S(2)}) copy-start(bf16[256,1024]{1,0:T(8,128)(2,1)} %param.8) | copy-start | bytes 1572868
  72.0 0.7 copy-start.4
  72.0 4.0 %copy-start.3 = (bf16[16,1024]{1,0:T(8,128)(2,1)S(1)}, bf16[16,1024]{1,0:T(8,128)(2,1)}, u32[]{:S(2)}) copy-start(bf16[16,1024]{1,0:T(8,128)(2,1)} %param.9) | copy-start | bytes 98308
Sparse Core Ops, SparseCore 0:
  9.6 48.3 all-gather.1
  72.1 112.3 all-reduce.1
where the time goes:
time: 194 us; the launch traced here: 193 us
  waiting for transfers between devices  126 us (65%)
  blocking collectives  23.5 us (12%)
  between operations  14.8 us (8%)
  matrix products  12.6 us (6%)
  local copies, waits for them, and re-layouts  9.73 us (5%)
  other arithmetic  7.09 us (4%)
    psum x1, waiting for transfers between devices, body(): summed = lax.psum(term, ('queue', 'dp'))  78.9 us
    all_gather x1, waiting for transfers between devices, body(): lax.all_gather(queue_keys, 'queue', axis=0, tiled=True)  46.1 us
    all_gather x1, blocking collectives, body(): arrived = lax.all_gather(fresh, ('queue', 'dp'), axis=0, tiled=True)  23.5 us
    gather x1, local copies, waits for them, and re-layouts, fold(): jnp.take(piece, jnp.clip(mapped, 0, count - 1), axis=0).astype(jnp.float32)  4.21 us
  transfers between devices with their start and end apart: 2, of which 2 were waited for; matrix products, arithmetic and copies ran while one was open for 7% of the time, Pallas kernels for 0%

commit v1 on v0

--- a/solution.py
+++ b/solution.py
@@ -74,7 +74,7 @@
     term = lax.dot_general(
         query_inputs, grad_query, (((0,), (0,)), ((), ())), preferred_element_type=jnp.float32
     )
-    summed = lax.psum(term, ("queue", "dp"))
+    summed = jnp.sum(lax.all_gather(term, ("queue", "dp")), 0)
     grad_rows = lax.dynamic_slice_in_dim(summed, lax.axis_index(("queue", "dp")) * share, share, 0)
     fresh = jnp.dot(key_inputs, key_weight, preferred_element_type=jnp.float32)
     fresh = (fresh * lax.rsqrt(jnp.sum(fresh * fresh, -1, keepdims=True) + 1e-06)).astype(

time: 194 us -> 500 us (2.58)
  waiting for transfers between devices: 126 us -> 343 us
  local copies, waits for them, and re-layouts: 9.73 us -> 75 us
  other arithmetic: 7.09 us -> 30.5 us
    all_gather x0 -> x1, waiting for transfers between devices: none -> 295 us  [body(): summed = jnp.sum(lax.all_gather(term, ('queue', 'dp')), 0)]
    psum x1 -> x0, waiting for transfers between devices: 78.9 us -> none  [body(): summed = lax.psum(term, ('queue', 'dp'))]
    unnamed x11 -> x12, local copies, waits for them, and re-layouts: 2.51 us -> 67.7 us
    reduce_sum x0 -> x1, other arithmetic: none -> 23.4 us  [body(): summed = jnp.sum(lax.all_gather(term, ('queue', 'dp')), 0)]
  transfers between devices with their start and end apart: 2 -> 2, of which waited for: 2 -> 2; matrix products, arithmetic and copies ran while one was open for 7% -> 3% of each run, Pallas kernels for 0% -> 0%
where the time goes in v1:
time: 500 us; the launch traced here: 499 us
  waiting for transfers between devices  343 us (69%)
  local copies, waits for them, and re-layouts  75 us (15%)
  other arithmetic  30.5 us (6%)
  blocking collectives  23.7 us (5%)
  between operations  14.8 us (3%)
  matrix products  12.6 us (3%)
    all_gather x1, waiting for transfers between devices, body(): summed = jnp.sum(lax.all_gather(term, ('queue', 'dp')), 0)  295 us
    unnamed x12, local copies, waits for them, and re-layouts  67.7 us
    all_gather x1, waiting for transfers between devices, body(): lax.all_gather(queue_keys, 'queue', axis=0, tiled=True)  46.8 us
    all_gather x1, blocking collectives, body(): arrived = lax.all_gather(fresh, ('queue', 'dp'), axis=0, tiled=True)  23.7 us
    reduce_sum x1, other arithmetic, body(): summed = jnp.sum(lax.all_gather(term, ('queue', 'dp')), 0)  23.4 us
  transfers between devices with their start and end apart: 2, of which 2 were waited for; matrix products, arithmetic and copies ran while one was open for 3% of the time, Pallas kernels for 0%

profile of v1, /device:TPU:0, one launch (start us, length us, event | category | flops | bytes accessed | tf_op | source)
XLA Modules:
  0.0 499.4 jit_solution(13609010783588823303)
XLA Ops:
  7.2 0.0 copy-start
  7.2 0.0 all-gather.4.cloned.1.call-start
  7.2 0.7 all-gather.4.cloned.1.call-update
  7.9 0.0 all-gather.6.cloned.1.call-start
  8.0 0.7 compare_select_fusion.9
  8.7 0.7 compare_and_fusion.1
  9.3 0.0 copy-done
  9.3 1.8 multiply_reduce_fusion.2
  11.2 46.8 %all-gather.4.cloned.1.call-done = bf16[1024,1024]{1,0:T(8,128)(2,1)} async-done(((bf16[256,1024]{1,0:T(8,128)(2,1)}), bf16[1024,1024]{1,0:T(8,128)(2,1)}) %all-gather.4.cloned.1.call-update) | async-done | bytes 2097168 | tf_op jit(solution)/shard_map/all_gather | solution.py:62
  58.0 2.4 fusion.14
  60.4 0.0 copy-start.1
  60.4 1.0 copy-done.1
  61.4 0.3 fusion.3
  61.7 4.2 gather_fusion
  65.9 0.0 copy-start.2
  65.9 3.1 multiply_reduce_fusion
  69.0 0.0 copy-done.2
  69.0 3.0 convolution_bitcast_fusion
  72.0 0.0 copy-start.4
  72.0 0.0 copy-start.3
  72.0 0.0 all-gather.6.cloned.1.call-update
  72.7 0.0 copy-done.4
  72.7 0.2 select_reduce_fusion
  72.9 0.7 fusion.13
  73.5 2.6 compare_select_fusion
  76.1 0.0 copy-done.3
  76.1 2.2 multiply_reduce_fusion.3
  78.4 0.1 multiply_convert_fusion.3
  78.5 23.7 %all_gather.15 = bf16[256,1024]{1,0:T(8,128)(2,1)S(1)} all-gather(bf16[16,1024]{1,0:T(8,128)(2,1)S(1)} %multiply_convert_fusion.3), channel_id=1, replica_groups=mesh['groups'=2,'queue'=4,'dp'=4] {'queue','dp'}, dimensions={0}, use_global_device_ids=true | all-gather | bytes 557056 | tf_op jit(solution)/shard_map/all_gather | solution.py:83
  102.1 1.2 gather_fusion.1
  103.3 2.0 select_select_fusion
  105.3 0.6 multiply_subtract_fusion
  105.9 295.3 %all-gather.6.cloned.1.call-done = f32[16384,1024]{0,1:T(8,128)} async-done(((f32[1024,1024]{0,1:T(8,128)}), f32[16384,1024]{0,1:T(8,128)}) %all-gather.6.cloned.1.call-update) | async-done | bytes 67108880 | tf_op jit(solution)/shard_map/all_gather | solution.py:77
  401.2 65.8 %copy.13 = f32[128,8,16,1024]{3,2,1,0:T(8,128)} copy(f32[128,8,16,1024]{3,1,2,0:T(8,128)} %bitcast.9) | data formatting | bytes 134217728
  467.1 23.4 %bitcast_reduce_fusion = f32[1024,1024]{0,1:T(8,128)} fusion(f32[128,8,16,1024]{3,2,1,0:T(8,128)} %copy.13), kind=kLoop, calls=%fused_computation.2 | loop fusion | flops 15728640 | bytes 71303168 | tf_op jit(solution)/shard_map/reduce_sum | solution.py:77
  490.4 1.2 constant_dynamic-slice_fusion
  491.7 0.9 copy.12
  (7 shorter events, 0.1 us)
Async XLA Ops:
  7.2 2.2 copy-start
  7.2 50.8 %all-gather.4.cloned.1.call-start = ((), (), s32[]{:S(2)}) async-start(), calls=%async_computation | async-start | bytes 2621440 | tf_op jit(solution)/shard_map/all_gather | solution.py:62
  7.9 393.3 %all-gather.6.cloned.1.call-start = ((), (), s32[]{:S(2)}) async-start(), calls=%async_computation.1 | async-start | bytes 71303168 | tf_op jit(solution)/shard_map/all_gather | solution.py:77
  60.4 1.0 copy-start.1
  65.9 3.1 copy-start.2
  72.0 0.7 copy-start.4
  72.0 4.2 copy-start.3
Sparse Core Ops, SparseCore 0:
  9.6 48.3 all-gather.3
  72.1 329.0 all-gather.5
